TPU v7x, 512 devices: a whole 4x4x16 slice. The times are simulated.
512 devices in a mesh: gx: 64 (over z, y), gy: 8 (over x, core).
Axes of the slice: x: 4, y: 4, z: 16, core: 2. Of those that a mesh axis runs over, the one named last changes fastest.
Arguments:
- rhs: float32 [64, 8, 128, 128], P('gx', 'gy'), may hold values from -57 to 57
- face_rows: int32 [64, 8, 4, 128], P('gx', 'gy'), may hold values from 0 to 127
- margin_weight: float32 [64, 8, 4, 128], P('gx', 'gy'), may hold values from 0.2 to 1
- local_blocks: bfloat16 [64, 8, 1, 128, 128], P('gx', 'gy'), may hold values from -0.4 to 4.4
- subdomain_inverse: bfloat16 [64, 8, 128, 640], P('gx', 'gy'), may hold values from -0.4 to 1.8
- coarse_basis: bfloat16 [64, 8, 128, 32], P('gx', 'gy'), may hold values from -0.5 to 0.5
- coarse_inverse: bfloat16 [64, 8, 32, 16384], P('gx', 'gy'), may hold values from -0.09765625 to 0.09765625
- coarse_map: int32 [512], replicated, may hold values from 0 to 511, each once
Outputs:
- solution: float32 [64, 8, 128, 128], P('gx', 'gy')
- relative_residual: float32 [128], replicated
Inputs may be any that keep to these rules, and one draw needn't show every extreme that they name: `face_rows`: rows of the subdomain, repeats possible. `coarse_map`: every position once.
All inputs are finite; a program needn't handle non-finite values.
Results may differ from a plain program's by a relative error of at most 0.004.
Values may be sent and summed in bfloat16 or wider, within the bound.
No kernel may reach another device: no remote copies, remote signals or barrier semaphores. Data moves between devices by JAX's collectives and lax.ppermute only.
A program may use at most 64 MiB of HBM per device.

v0:
```python
import jax
import jax.numpy as jnp
from jax import lax
from jax.sharding import PartitionSpec as P

EPSILON = 1e-06


def neighbours(rows, axis):
    count = lax.axis_size(axis)
    up = [(i, i + 1) for i in range(count - 1)]
    down = [(i + 1, i) for i in range(count - 1)]
    return (lax.ppermute(rows[1], axis, up), lax.ppermute(rows[0], axis, down))


def exchange(packs):
    below_first, above_first = neighbours(packs[0:2], "gx")
    below_second, above_second = neighbours(packs[2:4], "gy")
    return jnp.stack([below_first, above_first, below_second, above_second], axis=0)


def allsum(value):
    for axis in ("gy", "gx"):
        count = lax.axis_size(axis)
        if count & count - 1:
            value = lax.psum(value, axis)
            continue
        step = 1
        while step < count:
            value = value + lax.ppermute(value, axis, [(i, i ^ step) for i in range(count)])
            step *= 2
    return value


def least_squares(scale_norm, first_dot, first_norm, cross_dot, second_dot, second_norm):
    radius_one = jnp.sqrt(first_dot * first_dot + first_norm * first_norm)
    cosine_one = first_dot / radius_one
    sine_one = first_norm / radius_one
    upper_entry = cosine_one * cross_dot + sine_one * second_dot
    lower_entry = cosine_one * second_dot - sine_one * cross_dot
    radius_two = jnp.sqrt(lower_entry * lower_entry + second_norm * second_norm)
    cosine_two = lower_entry / radius_two
    sine_two = second_norm / radius_two
    weight_two = -cosine_two * sine_one * scale_norm / radius_two
    weight_one = (cosine_one * scale_norm - upper_entry * weight_two) / radius_one
    return (weight_one, weight_two, sine_one * sine_two)


def on_device(
    rhs,
    face_rows,
    margin_weight,
    local_blocks,
    subdomain_inverse,
    coarse_basis,
    coarse_inverse,
    coarse_map,
):
    right_side = rhs[0, 0]
    margin_rows = face_rows[0, 0]
    margin_weights = margin_weight[0, 0]
    local_block = local_blocks[0, 0]
    inverse_rows = subdomain_inverse[0, 0]
    basis = coarse_basis[0, 0]
    coarse_rows = coarse_inverse[0, 0]
    owned_rows = right_side.shape[0]
    system_count = right_side.shape[1]
    basis_count = basis.shape[1]
    block_rows = local_block.shape[1]
    count_x = lax.axis_size("gx")
    count_y = lax.axis_size("gy")
    gathered_map = coarse_map.reshape(count_x, count_y).T.reshape(-1)
    positions = (
        gathered_map[:, None] * basis_count + jnp.arange(basis_count, dtype=jnp.int32)[None, :]
    ).reshape(-1)
    permuted = jnp.take(coarse_rows, positions, axis=1)

    def margin_of(field):
        return exchange(field[margin_rows])

    def coarse_gather(residual):
        return lax.all_gather(
            lax.all_gather(residual, "gx", axis=0, tiled=True), "gy", axis=0, tiled=True
        )

    def precondition(rounded, margin):
        extended = jnp.concatenate([rounded, margin.reshape(-1, system_count)], axis=0)
        local_part = jnp.dot(inverse_rows, extended, preferred_element_type=jnp.float32)
        residual = lax.dot_general(
            basis, rounded, (((0,), (0,)), ((), ())), preferred_element_type=jnp.float32
        ).astype(jnp.bfloat16)
        solved = jnp.dot(permuted, coarse_gather(residual), preferred_element_type=jnp.float32)
        return local_part + jnp.dot(
            basis, solved.astype(jnp.bfloat16), preferred_element_type=jnp.float32
        )

    def apply_operator(vector):
        rounded = vector.astype(jnp.bfloat16)
        own_part = jnp.einsum(
            "brc,bcn->brn",
            local_block,
            rounded.reshape(-1, block_rows, system_count),
            preferred_element_type=jnp.float32,
        ).reshape(owned_rows, system_count)
        weighted = margin_weights[:, :, None] * margin_of(rounded).astype(jnp.float32)
        coupling = (
            jnp.zeros((owned_rows, system_count), jnp.float32)
            .at[margin_rows.reshape(-1)]
            .add(weighted.reshape(-1, system_count))
        )
        return own_part - coupling

    def column_norm(vector):
        return jnp.sqrt(allsum(jnp.sum(vector * vector, axis=0)) + EPSILON)

    rhs_margin = margin_of(right_side)
    scale_norm = column_norm(right_side)
    krylov_one = right_side / scale_norm
    margin_one = rhs_margin / scale_norm
    precond_one = precondition(krylov_one.astype(jnp.bfloat16), margin_one.astype(jnp.bfloat16))
    applied = apply_operator(precond_one)
    applied_margin = margin_of(applied)
    first_dot = allsum(jnp.sum(applied * krylov_one, axis=0))
    remainder = applied - first_dot * krylov_one
    first_norm = column_norm(remainder)
    krylov_two = remainder / first_norm
    margin_two = (applied_margin - first_dot * margin_one) / first_norm
    precond_two = precondition(krylov_two.astype(jnp.bfloat16), margin_two.astype(jnp.bfloat16))
    applied = apply_operator(precond_two)
    dots = allsum(
        jnp.stack([jnp.sum(applied * krylov_one, axis=0), jnp.sum(applied * krylov_two, axis=0)])
    )
    cross_dot = dots[0]
    second_dot = dots[1]
    remainder = applied - cross_dot * krylov_one - second_dot * krylov_two
    second_norm = column_norm(remainder)
    weight_one, weight_two, relative = least_squares(
        scale_norm, first_dot, first_norm, cross_dot, second_dot, second_norm
    )
    solution = weight_one * precond_one + weight_two * precond_two
    return (solution[None, None], relative)


def solution(mesh):
    return jax.shard_map(
        on_device,
        mesh=mesh,
        in_specs=(
            P("gx", "gy", None, None),
            P("gx", "gy", None, None),
            P("gx", "gy", None, None),
            P("gx", "gy", None, None, None),
            P("gx", "gy", None, None),
            P("gx", "gy", None, None),
            P("gx", "gy", None, None),
            P(),
        ),
        out_specs=(P("gx", "gy", None, None), P()),
        check_vma=False,
    )
```

profile of v0, /device:TPU:2, one launch (start us, length us, event | category | flops | bytes accessed | tf_op | source)
XLA Modules:
  0.0 728.0 jit_solution(14645991461228601917)
XLA Ops:
  11.3 7.8 %collective-permute-start.1 = (f32[128]{0:T(128)S(1)}, f32[128]{0:T(128)S(1)}, u32[]{:S(2)}, u32[]{:S(2)}) collective-permute-start(f32[128]{0:T(128)S(1)} %add.245), channel_id=1, source_target_pairs={{0,2},{1,3},{2,0},{3,1},{4,6},{5,7},{6,4},{7,5},{8,10},{9,11},{10,... | collective-permute-start | bytes 1544 | tf_op jit(solution)/shard_map/ppermute | solution.py:30
  22.5 5.0 collective-permute-done.2
  29.5 3.5 collective-permute-done.3
  34.9 5.0 collective-permute-done.4
  41.9 3.5 collective-permute-done.5
  47.3 4.4 collective-permute-done.6
  51.8 5.6 collective-permute-start.7
  57.3 3.8 collective-permute-done.7
  61.1 11.8 %collective-permute-start.8 = (f32[128]{0:T(128)S(1)}, f32[128]{0:T(128)S(1)}, u32[]{:S(2)}, u32[]{:S(2)}) collective-permute-start(f32[128]{0:T(128)S(1)} %add.252), channel_id=1, source_target_pairs={{0,256},{8,264},{16,272},{24,280},{32,288},{40,296},{48,304},{56,3... | collective-permute-start | bytes 1544 | tf_op jit(solution)/shard_map/ppermute | solution.py:30
  76.3 111.9 %all_gather.12 = bf16[2048,128]{1,0:T(8,128)(2,1)} all-gather(bf16[32,128]{1,0:T(8,128)(2,1)S(1)} %fusion.6), channel_id=1, replica_groups=mesh['gx'=64,'gy'=8] {'gx'}, dimensions={0}, use_global_device_ids=true | all-gather | bytes 532480 | tf_op jit(solution)/shard_map/all_gather | solution.py:83
  196.7 3.6 collective-permute-start.12
  204.4 58.2 %gather_fusion.1 = bf16[16384,32]{1,0:T(8,128)(2,1)} fusion(bf16[32,16384]{0,1:T(8,128)(2,1)} %bitcast.133, s32[16384]{0:T(1024)S(1)} %broadcast_clamp_fusion), kind=kCustom, calls=%fused_computation.1 | custom fusion | bytes 2162688 | tf_op jit(solution)/shard_map/jit(_take)/gather | solution.py:76
  263.1 7.1 convolution_add_fusion.1
  271.6 4.3 collective-permute-start.13
  279.2 3.6 collective-permute-start.16
  287.1 3.5 collective-permute-start.17
  299.6 4.2 collective-permute-done.19
  303.8 4.3 collective-permute-start.20
  309.6 6.4 collective-permute-start.21
  317.5 7.1 collective-permute-start.22
  326.2 3.8 collective-permute-start.23
  332.5 8.3 %collective-permute-start.24 = (f32[128]{0:T(128)S(1)}, f32[128]{0:T(128)S(1)}, u32[]{:S(2)}, u32[]{:S(2)}) collective-permute-start(f32[128]{0:T(128)S(1)} %add.273), channel_id=1, source_target_pairs={{0,128},{8,136},{16,144},{24,152},{32,160},{40,168},{48,176},{56,1... | collective-permute-start | bytes 1544 | tf_op jit(solution)/shard_map/ppermute | solution.py:30
  342.4 11.4 %collective-permute-start.25 = (f32[128]{0:T(128)S(1)}, f32[128]{0:T(128)S(1)}, u32[]{:S(2)}, u32[]{:S(2)}) collective-permute-start(f32[128]{0:T(128)S(1)} %add.274), channel_id=1, source_target_pairs={{0,256},{8,264},{16,272},{24,280},{32,288},{40,296},{48,304},{56,3... | collective-permute-start | bytes 1544 | tf_op jit(solution)/shard_map/ppermute | solution.py:30
  367.9 4.2 collective-permute-done.28
  374.0 3.5 collective-permute-done.29
  379.5 5.0 collective-permute-done.30
  384.5 3.4 collective-permute-start.31
  396.3 7.8 %collective-permute-start.33 = (f32[128]{0:T(128)S(1)}, f32[128]{0:T(128)S(1)}, u32[]{:S(2)}, u32[]{:S(2)}) collective-permute-start(f32[128]{0:T(128)S(1)} %add.282), channel_id=1, source_target_pairs={{0,128},{8,136},{16,144},{24,152},{32,160},{40,168},{48,176},{56,1... | collective-permute-start | bytes 1544 | tf_op jit(solution)/shard_map/ppermute | solution.py:30
  405.7 11.4 %collective-permute-start.34 = (f32[128]{0:T(128)S(1)}, f32[128]{0:T(128)S(1)}, u32[]{:S(2)}, u32[]{:S(2)}) collective-permute-start(f32[128]{0:T(128)S(1)} %add.283), channel_id=1, source_target_pairs={{0,256},{8,264},{16,272},{24,280},{32,288},{40,296},{48,304},{56,3... | collective-permute-start | bytes 1544 | tf_op jit(solution)/shard_map/ppermute | solution.py:30
  420.0 108.2 %all_gather.14 = bf16[2048,128]{1,0:T(8,128)(2,1)} all-gather(bf16[32,128]{1,0:T(8,128)(2,1)S(1)} %fusion.7), channel_id=1, replica_groups=mesh['gx'=64,'gy'=8] {'gx'}, dimensions={0}, use_global_device_ids=true | all-gather | bytes 532480 | tf_op jit(solution)/shard_map/all_gather | solution.py:83
  529.3 3.5 collective-permute-start.35
  536.2 3.6 collective-permute-start.38
  542.1 22.8 %all-gather.5.cloned.1.call-done = bf16[16384,128]{1,0:T(8,128)(2,1)} async-done(((bf16[2048,128]{1,0:T(8,128)(2,1)}), bf16[16384,128]{1,0:T(8,128)(2,1)}) %all-gather.5.cloned.1.call-update) | async-done | bytes 4194320 | tf_op jit(solution)/shard_map/all_gather | solution.py:82
  564.8 7.1 convolution_add_fusion
  573.4 3.4 collective-permute-start.39
  580.0 3.6 collective-permute-start.42
  599.6 4.7 collective-permute-done.45
  604.3 4.3 collective-permute-start.46
  610.1 5.4 collective-permute-start.47
  617.1 6.1 collective-permute-start.48
  624.7 4.9 collective-permute-start.49
  631.2 9.2 %collective-permute-start.50 = (f32[2,128]{1,0:T(2,128)S(1)}, f32[2,128]{1,0:T(2,128)S(1)}, u32[]{:S(2)}, u32[]{:S(2)}) collective-permute-start(f32[2,128]{1,0:T(2,128)S(1)} %add.294), channel_id=1, source_target_pairs={{0,128},{8,136},{16,144},{24,152},{32,160},{40,168},{48,176},{56,1... | collective-permute-start | bytes 3080 | tf_op jit(solution)/shard_map/ppermute | solution.py:30
  641.9 13.0 %collective-permute-start.51 = (f32[2,128]{1,0:T(2,128)S(1)}, f32[2,128]{1,0:T(2,128)S(1)}, u32[]{:S(2)}, u32[]{:S(2)}) collective-permute-start(f32[2,128]{1,0:T(2,128)S(1)} %add.295), channel_id=1, source_target_pairs={{0,256},{8,264},{16,272},{24,280},{32,288},{40,296},{48,304},{56,3... | collective-permute-start | bytes 3080 | tf_op jit(solution)/shard_map/ppermute | solution.py:30
  667.3 4.7 collective-permute-done.54
  673.9 3.5 collective-permute-done.55
  679.4 5.0 collective-permute-done.56
  696.2 7.5 %collective-permute-start.59 = (f32[128]{0:T(128)S(1)}, f32[128]{0:T(128)S(1)}, u32[]{:S(2)}, u32[]{:S(2)}) collective-permute-start(f32[128]{0:T(128)S(1)} %add.304), channel_id=1, source_target_pairs={{0,128},{8,136},{16,144},{24,152},{32,160},{40,168},{48,176},{56,1... | collective-permute-start | bytes 1544 | tf_op jit(solution)/shard_map/ppermute | solution.py:30
  705.6 12.6 %collective-permute-start.60 = (f32[128]{0:T(128)S(1)}, f32[128]{0:T(128)S(1)}, u32[]{:S(2)}, u32[]{:S(2)}) collective-permute-start(f32[128]{0:T(128)S(1)} %add.305), channel_id=1, source_target_pairs={{0,256},{8,264},{16,272},{24,280},{32,288},{40,296},{48,304},{56,3... | collective-permute-start | bytes 1544 | tf_op jit(solution)/shard_map/ppermute | solution.py:30
  (196 shorter events, 156.1 us)
Async XLA Ops:
  7.2 255.8 %all-gather.3.cloned.1.call-start = ((), (), s32[]{:S(2)}) async-start(), calls=%async_computation | async-start | bytes 4718592 | tf_op jit(solution)/shard_map/all_gather | solution.py:82
  11.3 9.3 %collective-permute-start.1 = (f32[128]{0:T(128)S(1)}, f32[128]{0:T(128)S(1)}, u32[]{:S(2)}, u32[]{:S(2)}) collective-permute-start(f32[128]{0:T(128)S(1)} %add.245), channel_id=1, source_target_pairs={{0,2},{1,3},{2,0},{3,1},{4,6},{5,7},{6,4},{7,5},{8,10},{9,11},{10,... | collective-permute-start | bytes 1544 | tf_op jit(solution)/shard_map/ppermute | solution.py:30
  20.6 7.0 collective-permute-start.2
  27.5 5.5 collective-permute-start.3
  33.0 7.0 collective-permute-start.4
  45.4 6.3 collective-permute-start.6
  51.8 9.4 %collective-permute-start.7 = (f32[128]{0:T(128)S(1)}, f32[128]{0:T(128)S(1)}, u32[]{:S(2)}, u32[]{:S(2)}) collective-permute-start(f32[128]{0:T(128)S(1)} %add.251), channel_id=1, source_target_pairs={{0,128},{8,136},{16,144},{24,152},{32,160},{40,168},{48,176},{56,1... | collective-permute-start | bytes 1544 | tf_op jit(solution)/shard_map/ppermute | solution.py:30
  61.1 14.2 %collective-permute-start.8 = (f32[128]{0:T(128)S(1)}, f32[128]{0:T(128)S(1)}, u32[]{:S(2)}, u32[]{:S(2)}) collective-permute-start(f32[128]{0:T(128)S(1)} %add.252), channel_id=1, source_target_pairs={{0,256},{8,264},{16,272},{24,280},{32,288},{40,296},{48,304},{56,3... | collective-permute-start | bytes 1544 | tf_op jit(solution)/shard_map/ppermute | solution.py:30
  188.2 376.6 %all-gather.5.cloned.1.call-start = ((), (), s32[]{:S(2)}) async-start(), calls=%async_computation.1 | async-start | bytes 4718592 | tf_op jit(solution)/shard_map/all_gather | solution.py:82
  190.9 71.8 %collective-permute-start.9 = (f32[128,128]{1,0:T(8,128)S(1)}, f32[128,128]{1,0:T(8,128)S(1)}, u32[]{:S(2)}, u32[]{:S(2)}) collective-permute-start(f32[128,128]{1,0:T(8,128)S(1)} %get-tuple-element.19), channel_id=1, source_target_pairs={{0,8},{8,16},{16,24},{24,32},{32,40},{40,48},{48,56},{56,64},{64,7... | collective-permute-start | bytes 196616 | tf_op jit(solution)/shard_map/ppermute | solution.py:13
  193.5 69.1 %collective-permute-start.11 = (f32[128,128]{1,0:T(8,128)S(1)}, f32[128,128]{1,0:T(8,128)S(1)}, u32[]{:S(2)}, u32[]{:S(2)}) collective-permute-start(f32[128,128]{1,0:T(8,128)S(1)} %get-tuple-element.20), channel_id=1, source_target_pairs={{0,1},{1,2},{2,3},{3,4},{4,5},{5,6},{6,7},{8,9},{9,10},{10,11},{11... | collective-permute-start | bytes 196616 | tf_op jit(solution)/shard_map/ppermute | solution.py:13
  195.4 67.2 %collective-permute-start.10 = (f32[128,128]{1,0:T(8,128)S(1)}, f32[128,128]{1,0:T(8,128)S(1)}, u32[]{:S(2)}, u32[]{:S(2)}) collective-permute-start(f32[128,128]{1,0:T(8,128)S(1)} %get-tuple-element.21), channel_id=1, source_target_pairs={{8,0},{16,8},{24,16},{32,24},{40,32},{48,40},{56,48},{64,56},{72,6... | collective-permute-start | bytes 196616 | tf_op jit(solution)/shard_map/ppermute | solution.py:13
  196.7 65.9 %collective-permute-start.12 = (f32[128,128]{1,0:T(8,128)S(1)}, f32[128,128]{1,0:T(8,128)S(1)}, u32[]{:S(2)}, u32[]{:S(2)}) collective-permute-start(f32[128,128]{1,0:T(8,128)S(1)} %get-tuple-element.22), channel_id=1, source_target_pairs={{1,0},{2,1},{3,2},{4,3},{5,4},{6,5},{7,6},{9,8},{10,9},{11,10},{12... | collective-permute-start | bytes 196616 | tf_op jit(solution)/shard_map/ppermute | solution.py:13
  271.6 11.2 %collective-permute-start.13 = (bf16[128,128]{1,0:T(8,128)(2,1)S(1)}, bf16[128,128]{1,0:T(8,128)(2,1)S(1)}, u32[]{:S(2)}, u32[]{:S(2)}) collective-permute-start(bf16[128,128]{1,0:T(8,128)(2,1)S(1)} %get-tuple-element.27), channel_id=1, source_target_pairs={{0,8},{8,16},{16,24},{24,32},{32,40},{40,48},{48,56},{56,64},{64,7... | collective-permute-start | bytes 98312 | tf_op jit(solution)/shard_map/ppermute | solution.py:13
  276.0 6.9 collective-permute-start.15
  277.9 5.8 collective-permute-start.14
  296.8 7.0 collective-permute-start.19
  303.8 5.8 collective-permute-start.20
  309.6 7.9 %collective-permute-start.21 = (f32[128]{0:T(128)S(1)}, f32[128]{0:T(128)S(1)}, u32[]{:S(2)}, u32[]{:S(2)}) collective-permute-start(f32[128]{0:T(128)S(1)} %add.270), channel_id=1, source_target_pairs={{0,16},{8,24},{16,0},{24,8},{32,48},{40,56},{48,32},{56,40},{64,80... | collective-permute-start | bytes 1544 | tf_op jit(solution)/shard_map/ppermute | solution.py:30
  317.5 8.7 %collective-permute-start.22 = (f32[128]{0:T(128)S(1)}, f32[128]{0:T(128)S(1)}, u32[]{:S(2)}, u32[]{:S(2)}) collective-permute-start(f32[128]{0:T(128)S(1)} %add.271), channel_id=1, source_target_pairs={{0,32},{8,40},{16,48},{24,56},{32,0},{40,8},{48,16},{56,24},{64,96... | collective-permute-start | bytes 1544 | tf_op jit(solution)/shard_map/ppermute | solution.py:30
  326.2 6.3 collective-permute-start.23
  332.5 9.9 %collective-permute-start.24 = (f32[128]{0:T(128)S(1)}, f32[128]{0:T(128)S(1)}, u32[]{:S(2)}, u32[]{:S(2)}) collective-permute-start(f32[128]{0:T(128)S(1)} %add.273), channel_id=1, source_target_pairs={{0,128},{8,136},{16,144},{24,152},{32,160},{40,168},{48,176},{56,1... | collective-permute-start | bytes 1544 | tf_op jit(solution)/shard_map/ppermute | solution.py:30
  342.4 14.2 %collective-permute-start.25 = (f32[128]{0:T(128)S(1)}, f32[128]{0:T(128)S(1)}, u32[]{:S(2)}, u32[]{:S(2)}) collective-permute-start(f32[128]{0:T(128)S(1)} %add.274), channel_id=1, source_target_pairs={{0,256},{8,264},{16,272},{24,280},{32,288},{40,296},{48,304},{56,3... | collective-permute-start | bytes 1544 | tf_op jit(solution)/shard_map/ppermute | solution.py:30
  365.1 7.0 collective-permute-start.28
  377.6 7.0 collective-permute-start.30
  390.0 6.3 collective-permute-start.32
  396.3 9.4 %collective-permute-start.33 = (f32[128]{0:T(128)S(1)}, f32[128]{0:T(128)S(1)}, u32[]{:S(2)}, u32[]{:S(2)}) collective-permute-start(f32[128]{0:T(128)S(1)} %add.282), channel_id=1, source_target_pairs={{0,128},{8,136},{16,144},{24,152},{32,160},{40,168},{48,176},{56,1... | collective-permute-start | bytes 1544 | tf_op jit(solution)/shard_map/ppermute | solution.py:30
  405.7 14.2 %collective-permute-start.34 = (f32[128]{0:T(128)S(1)}, f32[128]{0:T(128)S(1)}, u32[]{:S(2)}, u32[]{:S(2)}) collective-permute-start(f32[128]{0:T(128)S(1)} %add.283), channel_id=1, source_target_pairs={{0,256},{8,264},{16,272},{24,280},{32,288},{40,296},{48,304},{56,3... | collective-permute-start | bytes 1544 | tf_op jit(solution)/shard_map/ppermute | solution.py:30
  529.3 10.5 %collective-permute-start.35 = (f32[128,128]{1,0:T(8,128)S(1)}, f32[128,128]{1,0:T(8,128)S(1)}, u32[]{:S(2)}, u32[]{:S(2)}) collective-permute-start(f32[128,128]{1,0:T(8,128)S(1)} %get-tuple-element.15), channel_id=1, source_target_pairs={{0,8},{8,16},{16,24},{24,32},{32,40},{40,48},{48,56},{56,64},{64,7... | collective-permute-start | bytes 196616 | tf_op jit(solution)/shard_map/ppermute | solution.py:13
  532.8 7.1 collective-permute-start.37
  534.7 6.5 collective-permute-start.36
  536.2 5.5 collective-permute-start.38
  573.4 10.3 %collective-permute-start.39 = (bf16[128,128]{1,0:T(8,128)(2,1)S(1)}, bf16[128,128]{1,0:T(8,128)(2,1)S(1)}, u32[]{:S(2)}, u32[]{:S(2)}) collective-permute-start(bf16[128,128]{1,0:T(8,128)(2,1)S(1)} %get-tuple-element.23), channel_id=1, source_target_pairs={{0,8},{8,16},{16,24},{24,32},{32,40},{40,48},{48,56},{56,64},{64,7... | collective-permute-start | bytes 98312 | tf_op jit(solution)/shard_map/ppermute | solution.py:13
  576.8 6.9 collective-permute-start.41
  578.7 5.9 collective-permute-start.40
  591.9 5.5 collective-permute-start.44
  597.3 7.0 collective-permute-start.45
  604.3 5.8 collective-permute-start.46
  610.1 7.0 collective-permute-start.47
  617.1 7.6 %collective-permute-start.48 = (f32[2,128]{1,0:T(2,128)S(1)}, f32[2,128]{1,0:T(2,128)S(1)}, u32[]{:S(2)}, u32[]{:S(2)}) collective-permute-start(f32[2,128]{1,0:T(2,128)S(1)} %add.292), channel_id=1, source_target_pairs={{0,32},{8,40},{16,48},{24,56},{32,0},{40,8},{48,16},{56,24},{64,96... | collective-permute-start | bytes 3080 | tf_op jit(solution)/shard_map/ppermute | solution.py:30
  624.7 6.4 collective-permute-start.49
  631.2 10.8 %collective-permute-start.50 = (f32[2,128]{1,0:T(2,128)S(1)}, f32[2,128]{1,0:T(2,128)S(1)}, u32[]{:S(2)}, u32[]{:S(2)}) collective-permute-start(f32[2,128]{1,0:T(2,128)S(1)} %add.294), channel_id=1, source_target_pairs={{0,128},{8,136},{16,144},{24,152},{32,160},{40,168},{48,176},{56,1... | collective-permute-start | bytes 3080 | tf_op jit(solution)/shard_map/ppermute | solution.py:30
  641.9 14.5 %collective-permute-start.51 = (f32[2,128]{1,0:T(2,128)S(1)}, f32[2,128]{1,0:T(2,128)S(1)}, u32[]{:S(2)}, u32[]{:S(2)}) collective-permute-start(f32[2,128]{1,0:T(2,128)S(1)} %add.295), channel_id=1, source_target_pairs={{0,256},{8,264},{16,272},{24,280},{32,288},{40,296},{48,304},{56,3... | collective-permute-start | bytes 3080 | tf_op jit(solution)/shard_map/ppermute | solution.py:30
  665.0 7.0 collective-permute-start.54
  677.5 7.0 collective-permute-start.56
  689.9 6.3 collective-permute-start.58
  696.2 9.4 %collective-permute-start.59 = (f32[128]{0:T(128)S(1)}, f32[128]{0:T(128)S(1)}, u32[]{:S(2)}, u32[]{:S(2)}) collective-permute-start(f32[128]{0:T(128)S(1)} %add.304), channel_id=1, source_target_pairs={{0,128},{8,136},{16,144},{24,152},{32,160},{40,168},{48,176},{56,1... | collective-permute-start | bytes 1544 | tf_op jit(solution)/shard_map/ppermute | solution.py:30
  705.6 14.2 %collective-permute-start.60 = (f32[128]{0:T(128)S(1)}, f32[128]{0:T(128)S(1)}, u32[]{:S(2)}, u32[]{:S(2)}) collective-permute-start(f32[128]{0:T(128)S(1)} %add.305), channel_id=1, source_target_pairs={{0,256},{8,264},{16,272},{24,280},{32,288},{40,296},{48,304},{56,3... | collective-permute-start | bytes 1544 | tf_op jit(solution)/shard_map/ppermute | solution.py:30
  (23 other events, 896.3 us)
Sparse Core Ops, SparseCore 0:
  188.4 33.9 all-gather.2
  528.4 36.4 all-gather.4
where the time goes:
time: 730 us; the launch traced here: 728 us
  starting transfers between devices  252 us (35%)
  blocking collectives  220 us (30%)
  waiting for transfers between devices  149 us (20%)
  local copies, waits for them, and re-layouts  68.5 us (9%)
  matrix products  16.1 us (2%)
  between operations  15 us (2%)
  other arithmetic  7.87 us (1%)
    all_gather x2, blocking collectives, coarse_gather(): lax.all_gather(residual, 'gx', axis=0, tiled=True)  220 us
    ppermute x45, starting transfers between devices, allsum(): lax.ppermute(value, axis, [(i, i ^ step) for i in range(count)])  210 us
    ppermute x45, waiting for transfers between devices, allsum(): lax.ppermute(value, axis, [(i, i ^ step) for i in range(count)])  121 us
    gather x1, local copies, waits for them, and re-layouts, on_device(): permuted = jnp.take(coarse_rows, positions, axis=1)  58.2 us
    ppermute x16, starting transfers between devices, neighbours(): return (lax.ppermute(rows[1], axis, up), lax.ppermute(rows[0], axis, down))  41.4 us
    all_gather x2, waiting for transfers between devices, coarse_gather(): lax.all_gather(lax.all_gather(residual, 'gx', axis=0, tiled=True), 'gy',...  22.8 us
  transfers between devices with their start and end apart: 63, of which 52 were waited for; matrix products, arithmetic and copies ran while one was open for 9% of the time, Pallas kernels for 0%

commit v1 on v0

--- a/solution.py
+++ b/solution.py
@@ -4,6 +4,27 @@
 from jax.sharding import PartitionSpec as P
 
 EPSILON = 1e-06
+
+
+def gather_around(x, axis, dim):
+    count, index, extent = (lax.axis_size(axis), lax.axis_index(axis), x.shape[dim])
+    forward = [(i, (i + 1) % count) for i in range(count)]
+    backward = [(i, (i - 1) % count) for i in range(count)]
+    out = jnp.zeros((*x.shape[:dim], count * extent, *x.shape[dim + 1 :]), x.dtype)
+    out = lax.dynamic_update_slice_in_dim(out, x, index * extent, axis=dim)
+    from_left = from_right = x
+    middle = count // 2
+    for step in range(1, middle + 1):
+        from_left = lax.ppermute(from_left, axis, forward)
+        out = lax.dynamic_update_slice_in_dim(
+            out, from_left, (index - step) % count * extent, axis=dim
+        )
+        if step < count - middle:
+            from_right = lax.ppermute(from_right, axis, backward)
+            out = lax.dynamic_update_slice_in_dim(
+                out, from_right, (index + step) % count * extent, axis=dim
+            )
+    return out
 
 
 def neighbours(rows, axis):
@@ -79,9 +100,7 @@
         return exchange(field[margin_rows])
 
     def coarse_gather(residual):
-        return lax.all_gather(
-            lax.all_gather(residual, "gx", axis=0, tiled=True), "gy", axis=0, tiled=True
-        )
+        return gather_around(lax.all_gather(residual, "gx", axis=0, tiled=True), "gy", 0)
 
     def precondition(rounded, margin):
         extended = jnp.concatenate([rounded, margin.reshape(-1, system_count)], axis=0)

time: 730 us -> 735 us (level)
  the two profiles are of different devices: /device:TPU:2 before, /device:TPU:32 now
where the time goes in v1:
time: 735 us; the launch traced here: 733 us
  starting transfers between devices  219 us (30%)
  blocking collectives  202 us (27%)
  waiting for transfers between devices  201 us (27%)
  local copies, waits for them, and re-layouts  86 us (12%)
  matrix products  15.2 us (2%)
  other arithmetic  8.54 us (1%)
    all_gather x2, blocking collectives, coarse_gather(): lax.all_gather(residual, 'gx', axis=0, tiled=True)  202 us
    ppermute x45, starting transfers between devices, allsum(): lax.ppermute(value, axis, [(i, i ^ step) for i in range(count)])  155 us
    ppermute x45, waiting for transfers between devices, allsum(): lax.ppermute(value, axis, [(i, i ^ step) for i in range(count)])  153 us
    gather x1, local copies, waits for them, and re-layouts, on_device(): permuted = jnp.take(coarse_rows, positions, axis=1)  57.6 us
    ppermute x16, starting transfers between devices, neighbours(): return (lax.ppermute(rows[1], axis, up), lax.ppermute(rows[0], axis, down))  46.6 us
    ppermute x6, waiting for transfers between devices, gather_around(): from_right = lax.ppermute(from_right, axis, backward)  19.7 us
    ppermute x6, starting transfers between devices, gather_around(): from_right = lax.ppermute(from_right, axis, backward)  16.4 us
  transfers between devices with their start and end apart: 75, of which 57 were waited for; matrix products, arithmetic and copies ran while one was open for 11% of the time, Pallas kernels for 0%

profile of v1, /device:TPU:32, one launch (start us, length us, event | category | flops | bytes accessed | tf_op | source)
XLA Modules:
  0.0 733.3 jit_solution(8799608200374896432)
XLA Ops:
  10.2 4.9 collective-permute-start.2
  22.6 5.1 collective-permute-start.4
  32.0 6.7 collective-permute-start.10
  48.9 3.6 collective-permute-done.6
  52.5 6.7 collective-permute-start.7
  61.9 12.1 %collective-permute-start.8 = (f32[128]{0:T(128)S(1)}, f32[128]{0:T(128)S(1)}, u32[]{:S(2)}, u32[]{:S(2)}) collective-permute-start(f32[128]{0:T(128)S(1)} %add.329), channel_id=1, source_target_pairs={{0,256},{8,264},{16,272},{24,280},{32,288},{40,296},{48,304},{56,3... | collective-permute-start | bytes 1544 | tf_op jit(solution)/shard_map/ppermute | solution.py:51
  76.2 103.5 %all_gather.6 = bf16[2048,128]{1,0:T(8,128)(2,1)S(1)} all-gather(bf16[32,128]{1,0:T(8,128)(2,1)S(1)} %fusion.6), channel_id=1, replica_groups=mesh['gx'=64,'gy'=8] {'gx'}, dimensions={0}, use_global_device_ids=true | all-gather | bytes 532480 | tf_op jit(solution)/shard_map/all_gather | solution.py:103
  183.0 57.6 %gather_fusion.1 = bf16[16384,32]{1,0:T(8,128)(2,1)} fusion(bf16[32,16384]{0,1:T(8,128)(2,1)} %bitcast.133, s32[16384]{0:T(1024)S(1)} %broadcast_clamp_fusion), kind=kCustom, calls=%fused_computation.1 | custom fusion | bytes 2162688 | tf_op jit(solution)/shard_map/jit(_take)/gather | solution.py:97
  246.9 6.6 collective-permute-done.14
  258.5 4.7 collective-permute-done.16
  268.9 4.1 collective-permute-done.18
  277.9 7.1 convolution_add_fusion.1
  290.8 4.6 collective-permute-start.21
  297.4 5.9 collective-permute-done.20
  316.4 5.0 collective-permute-done.26
  328.8 5.0 collective-permute-done.28
  341.5 4.2 collective-permute-done.30
  345.7 4.5 collective-permute-start.31
  350.1 4.9 collective-permute-done.31
  355.0 8.7 %collective-permute-start.32 = (f32[128]{0:T(128)S(1)}, f32[128]{0:T(128)S(1)}, u32[]{:S(2)}, u32[]{:S(2)}) collective-permute-start(f32[128]{0:T(128)S(1)} %add.369), channel_id=1, source_target_pairs={{0,256},{8,264},{16,272},{24,280},{32,288},{40,296},{48,304},{56,3... | collective-permute-start | bytes 1544 | tf_op jit(solution)/shard_map/ppermute | solution.py:51
  363.7 5.5 collective-permute-done.32
  379.7 5.0 collective-permute-done.35
  392.1 5.0 collective-permute-done.37
  404.7 4.2 collective-permute-done.39
  408.9 4.5 collective-permute-start.40
  413.4 4.9 collective-permute-done.40
  418.3 8.7 %collective-permute-start.41 = (f32[128]{0:T(128)S(1)}, f32[128]{0:T(128)S(1)}, u32[]{:S(2)}, u32[]{:S(2)}) collective-permute-start(f32[128]{0:T(128)S(1)} %add.378), channel_id=1, source_target_pairs={{0,256},{8,264},{16,272},{24,280},{32,288},{40,296},{48,304},{56,3... | collective-permute-start | bytes 1544 | tf_op jit(solution)/shard_map/ppermute | solution.py:51
  428.0 4.5 collective-permute-done.41
  432.6 98.2 %all_gather.7 = bf16[2048,128]{1,0:T(8,128)(2,1)S(1)} all-gather(bf16[32,128]{1,0:T(8,128)(2,1)S(1)} %fusion.7), channel_id=1, replica_groups=mesh['gx'=64,'gy'=8] {'gx'}, dimensions={0}, use_global_device_ids=true | all-gather | bytes 532480 | tf_op jit(solution)/shard_map/all_gather | solution.py:103
  535.2 4.6 collective-permute-start.43
  569.8 5.4 collective-permute-done.52
  576.1 7.1 convolution_add_fusion
  589.0 5.8 collective-permute-start.54
  596.7 6.0 collective-permute-done.53
  610.3 3.5 collective-permute-done.58
  615.8 5.0 collective-permute-done.59
  622.7 3.5 collective-permute-done.60
  628.2 5.0 collective-permute-done.61
  645.0 5.7 collective-permute-start.64
  650.7 3.7 collective-permute-done.64
  654.4 9.8 %collective-permute-start.65 = (f32[2,128]{1,0:T(2,128)S(1)}, f32[2,128]{1,0:T(2,128)S(1)}, u32[]{:S(2)}, u32[]{:S(2)}) collective-permute-start(f32[2,128]{1,0:T(2,128)S(1)} %add.390), channel_id=1, source_target_pairs={{0,256},{8,264},{16,272},{24,280},{32,288},{40,296},{48,304},{56,3... | collective-permute-start | bytes 3080 | tf_op jit(solution)/shard_map/ppermute | solution.py:51
  664.2 4.3 collective-permute-done.65
  679.1 5.0 collective-permute-done.68
  691.5 5.0 collective-permute-done.70
  708.3 5.7 collective-permute-start.73
  714.0 3.7 collective-permute-done.73
  717.7 9.8 %collective-permute-start.74 = (f32[128]{0:T(128)S(1)}, f32[128]{0:T(128)S(1)}, u32[]{:S(2)}, u32[]{:S(2)}) collective-permute-start(f32[128]{0:T(128)S(1)} %add.400), channel_id=1, source_target_pairs={{0,256},{8,264},{16,272},{24,280},{32,288},{40,296},{48,304},{56,3... | collective-permute-start | bytes 1544 | tf_op jit(solution)/shard_map/ppermute | solution.py:51
  727.5 4.3 collective-permute-done.74
  (234 shorter events, 222.6 us)
Async XLA Ops:
  10.2 7.0 collective-permute-start.2
  22.6 18.1 %collective-permute-start.4 = (f32[128]{0:T(128)S(1)}, f32[128]{0:T(128)S(1)}, u32[]{:S(2)}, u32[]{:S(2)}) collective-permute-start(f32[128]{0:T(128)S(1)} %add.325), channel_id=1, source_target_pairs={{0,16},{8,24},{16,0},{24,8},{32,48},{40,56},{48,32},{56,40},{64,80... | collective-permute-start | bytes 1544 | tf_op jit(solution)/shard_map/ppermute | solution.py:51
  27.7 216.1 %collective-permute-start.12 = (f32[128,128]{1,0:T(8,128)S(1)}, f32[128,128]{1,0:T(8,128)S(1)}, u32[]{:S(2)}, u32[]{:S(2)}) collective-permute-start(f32[128,128]{1,0:T(8,128)S(1)} %get-tuple-element.20), channel_id=1, source_target_pairs={{1,0},{2,1},{3,2},{4,3},{5,4},{6,5},{7,6},{9,8},{10,9},{11,10},{12... | collective-permute-start | bytes 196616 | tf_op jit(solution)/shard_map/ppermute | solution.py:34
  29.0 217.8 %collective-permute-start.11 = (f32[128,128]{1,0:T(8,128)S(1)}, f32[128,128]{1,0:T(8,128)S(1)}, u32[]{:S(2)}, u32[]{:S(2)}) collective-permute-start(f32[128,128]{1,0:T(8,128)S(1)} %get-tuple-element.18), channel_id=1, source_target_pairs={{0,1},{1,2},{2,3},{3,4},{4,5},{5,6},{6,7},{8,9},{9,10},{10,11},{11... | collective-permute-start | bytes 196616 | tf_op jit(solution)/shard_map/ppermute | solution.py:34
  32.0 214.8 %collective-permute-start.10 = (f32[128,128]{1,0:T(8,128)S(1)}, f32[128,128]{1,0:T(8,128)S(1)}, u32[]{:S(2)}, u32[]{:S(2)}) collective-permute-start(f32[128,128]{1,0:T(8,128)S(1)} %get-tuple-element.19), channel_id=1, source_target_pairs={{8,0},{16,8},{24,16},{32,24},{40,32},{48,40},{56,48},{64,56},{72,6... | collective-permute-start | bytes 196616 | tf_op jit(solution)/shard_map/ppermute | solution.py:34
  38.7 208.1 %collective-permute-start.9 = (f32[128,128]{1,0:T(8,128)S(1)}, f32[128,128]{1,0:T(8,128)S(1)}, u32[]{:S(2)}, u32[]{:S(2)}) collective-permute-start(f32[128,128]{1,0:T(8,128)S(1)} %get-tuple-element.17), channel_id=1, source_target_pairs={{0,8},{8,16},{16,24},{24,32},{32,40},{40,48},{48,56},{56,64},{64,7... | collective-permute-start | bytes 196616 | tf_op jit(solution)/shard_map/ppermute | solution.py:34
  52.5 9.4 %collective-permute-start.7 = (f32[128]{0:T(128)S(1)}, f32[128]{0:T(128)S(1)}, u32[]{:S(2)}, u32[]{:S(2)}) collective-permute-start(f32[128]{0:T(128)S(1)} %add.328), channel_id=1, source_target_pairs={{0,128},{8,136},{16,144},{24,152},{32,160},{40,168},{48,176},{56,1... | collective-permute-start | bytes 1544 | tf_op jit(solution)/shard_map/ppermute | solution.py:51
  61.9 14.2 %collective-permute-start.8 = (f32[128]{0:T(128)S(1)}, f32[128]{0:T(128)S(1)}, u32[]{:S(2)}, u32[]{:S(2)}) collective-permute-start(f32[128]{0:T(128)S(1)} %add.329), channel_id=1, source_target_pairs={{0,256},{8,264},{16,272},{24,280},{32,288},{40,296},{48,304},{56,3... | collective-permute-start | bytes 1544 | tf_op jit(solution)/shard_map/ppermute | solution.py:51
  179.7 67.1 %collective-permute-start.13 = (bf16[2048,128]{1,0:T(8,128)(2,1)S(1)}, bf16[2048,128]{1,0:T(8,128)(2,1)S(1)}, u32[]{:S(2)}, u32[]{:S(2)}) collective-permute-start(bf16[2048,128]{1,0:T(8,128)(2,1)S(1)} %all_gather.6), channel_id=1, source_target_pairs={{0,1},{1,2},{2,3},{3,4},{4,5},{5,6},{6,7},{7,0},{8,9},{9,10},{10,1... | collective-permute-start | bytes 1572872 | tf_op jit(solution)/shard_map/ppermute | solution.py:18
  243.7 9.7 %collective-permute-start.14 = (bf16[2048,128]{1,0:T(8,128)(2,1)S(1)}, bf16[2048,128]{1,0:T(8,128)(2,1)S(1)}, u32[]{:S(2)}, u32[]{:S(2)}) collective-permute-start(bf16[2048,128]{1,0:T(8,128)(2,1)S(1)} %all_gather.6), channel_id=1, source_target_pairs={{0,7},{1,0},{2,1},{3,2},{4,3},{5,4},{6,5},{7,6},{8,15},{9,8},{10,9... | collective-permute-start | bytes 1572872 | tf_op jit(solution)/shard_map/ppermute | solution.py:23
  246.8 10.0 %collective-permute-start.15 = (bf16[2048,128]{1,0:T(8,128)(2,1)S(1)}, bf16[2048,128]{1,0:T(8,128)(2,1)S(1)}, u32[]{:S(2)}, u32[]{:S(2)}) collective-permute-start(bf16[2048,128]{1,0:T(8,128)(2,1)S(1)} %collective-permute-done.13), channel_id=1, source_target_pairs={{0,1},{1,2},{2,3},{3,4},{4,5},{5,6},{6,7},{7,0},{8,9},{9,10},{10,1... | collective-permute-start | bytes 1572872 | tf_op jit(solution)/shard_map/ppermute | solution.py:18
  253.4 9.8 %collective-permute-start.16 = (bf16[2048,128]{1,0:T(8,128)(2,1)S(1)}, bf16[2048,128]{1,0:T(8,128)(2,1)S(1)}, u32[]{:S(2)}, u32[]{:S(2)}) collective-permute-start(bf16[2048,128]{1,0:T(8,128)(2,1)S(1)} %collective-permute-done.14), channel_id=1, source_target_pairs={{0,7},{1,0},{2,1},{3,2},{4,3},{5,4},{6,5},{7,6},{8,15},{9,8},{10,9... | collective-permute-start | bytes 1572872 | tf_op jit(solution)/shard_map/ppermute | solution.py:23
  256.8 10.4 %collective-permute-start.17 = (bf16[2048,128]{1,0:T(8,128)(2,1)S(1)}, bf16[2048,128]{1,0:T(8,128)(2,1)S(1)}, u32[]{:S(2)}, u32[]{:S(2)}) collective-permute-start(bf16[2048,128]{1,0:T(8,128)(2,1)S(1)} %collective-permute-done.15), channel_id=1, source_target_pairs={{0,1},{1,2},{2,3},{3,4},{4,5},{5,6},{6,7},{7,0},{8,9},{9,10},{10,1... | collective-permute-start | bytes 1572872 | tf_op jit(solution)/shard_map/ppermute | solution.py:18
  263.2 9.8 %collective-permute-start.18 = (bf16[2048,128]{1,0:T(8,128)(2,1)S(1)}, bf16[2048,128]{1,0:T(8,128)(2,1)S(1)}, u32[]{:S(2)}, u32[]{:S(2)}) collective-permute-start(bf16[2048,128]{1,0:T(8,128)(2,1)S(1)} %collective-permute-done.16), channel_id=1, source_target_pairs={{0,7},{1,0},{2,1},{3,2},{4,3},{5,4},{6,5},{7,6},{8,15},{9,8},{10,9... | collective-permute-start | bytes 1572872 | tf_op jit(solution)/shard_map/ppermute | solution.py:23
  267.2 9.8 %collective-permute-start.19 = (bf16[2048,128]{1,0:T(8,128)(2,1)S(1)}, bf16[2048,128]{1,0:T(8,128)(2,1)S(1)}, u32[]{:S(2)}, u32[]{:S(2)}) collective-permute-start(bf16[2048,128]{1,0:T(8,128)(2,1)S(1)} %collective-permute-done.17), channel_id=1, source_target_pairs={{0,1},{1,2},{2,3},{3,4},{4,5},{5,6},{6,7},{7,0},{8,9},{9,10},{10,1... | collective-permute-start | bytes 1572872 | tf_op jit(solution)/shard_map/ppermute | solution.py:18
  286.5 10.9 %collective-permute-start.23 = (bf16[128,128]{1,0:T(8,128)(2,1)S(1)}, bf16[128,128]{1,0:T(8,128)(2,1)S(1)}, u32[]{:S(2)}, u32[]{:S(2)}) collective-permute-start(bf16[128,128]{1,0:T(8,128)(2,1)S(1)} %get-tuple-element.28), channel_id=1, source_target_pairs={{1,0},{2,1},{3,2},{4,3},{5,4},{6,5},{7,6},{9,8},{10,9},{11,10},{12... | collective-permute-start | bytes 98312 | tf_op jit(solution)/shard_map/ppermute | solution.py:34
  287.8 9.6 %collective-permute-start.22 = (bf16[128,128]{1,0:T(8,128)(2,1)S(1)}, bf16[128,128]{1,0:T(8,128)(2,1)S(1)}, u32[]{:S(2)}, u32[]{:S(2)}) collective-permute-start(bf16[128,128]{1,0:T(8,128)(2,1)S(1)} %get-tuple-element.26), channel_id=1, source_target_pairs={{0,1},{1,2},{2,3},{3,4},{4,5},{5,6},{6,7},{8,9},{9,10},{10,11},{11... | collective-permute-start | bytes 98312 | tf_op jit(solution)/shard_map/ppermute | solution.py:34
  295.4 7.9 %collective-permute-start.20 = (bf16[128,128]{1,0:T(8,128)(2,1)S(1)}, bf16[128,128]{1,0:T(8,128)(2,1)S(1)}, u32[]{:S(2)}, u32[]{:S(2)}) collective-permute-start(bf16[128,128]{1,0:T(8,128)(2,1)S(1)} %get-tuple-element.25), channel_id=1, source_target_pairs={{0,8},{8,16},{16,24},{24,32},{32,40},{40,48},{48,56},{56,64},{64,7... | collective-permute-start | bytes 98312 | tf_op jit(solution)/shard_map/ppermute | solution.py:34
  314.5 7.0 collective-permute-start.26
  326.9 7.0 collective-permute-start.28
  345.7 9.4 %collective-permute-start.31 = (f32[128]{0:T(128)S(1)}, f32[128]{0:T(128)S(1)}, u32[]{:S(2)}, u32[]{:S(2)}) collective-permute-start(f32[128]{0:T(128)S(1)} %add.368), channel_id=1, source_target_pairs={{0,128},{8,136},{16,144},{24,152},{32,160},{40,168},{48,176},{56,1... | collective-permute-start | bytes 1544 | tf_op jit(solution)/shard_map/ppermute | solution.py:51
  355.0 14.2 %collective-permute-start.32 = (f32[128]{0:T(128)S(1)}, f32[128]{0:T(128)S(1)}, u32[]{:S(2)}, u32[]{:S(2)}) collective-permute-start(f32[128]{0:T(128)S(1)} %add.369), channel_id=1, source_target_pairs={{0,256},{8,264},{16,272},{24,280},{32,288},{40,296},{48,304},{56,3... | collective-permute-start | bytes 1544 | tf_op jit(solution)/shard_map/ppermute | solution.py:51
  377.7 7.0 collective-permute-start.35
  390.2 7.0 collective-permute-start.37
  408.9 9.4 %collective-permute-start.40 = (f32[128]{0:T(128)S(1)}, f32[128]{0:T(128)S(1)}, u32[]{:S(2)}, u32[]{:S(2)}) collective-permute-start(f32[128]{0:T(128)S(1)} %add.377), channel_id=1, source_target_pairs={{0,128},{8,136},{16,144},{24,152},{32,160},{40,168},{48,176},{56,1... | collective-permute-start | bytes 1544 | tf_op jit(solution)/shard_map/ppermute | solution.py:51
  418.3 14.2 %collective-permute-start.41 = (f32[128]{0:T(128)S(1)}, f32[128]{0:T(128)S(1)}, u32[]{:S(2)}, u32[]{:S(2)}) collective-permute-start(f32[128]{0:T(128)S(1)} %add.378), channel_id=1, source_target_pairs={{0,256},{8,264},{16,272},{24,280},{32,288},{40,296},{48,304},{56,3... | collective-permute-start | bytes 1544 | tf_op jit(solution)/shard_map/ppermute | solution.py:51
  530.8 15.0 %collective-permute-start.46 = (bf16[2048,128]{1,0:T(8,128)(2,1)S(1)}, bf16[2048,128]{1,0:T(8,128)(2,1)S(1)}, u32[]{:S(2)}, u32[]{:S(2)}) collective-permute-start(bf16[2048,128]{1,0:T(8,128)(2,1)S(1)} %all_gather.7), channel_id=1, source_target_pairs={{0,1},{1,2},{2,3},{3,4},{4,5},{5,6},{6,7},{7,0},{8,9},{9,10},{10,1... | collective-permute-start | bytes 1572872 | tf_op jit(solution)/shard_map/ppermute | solution.py:18
  530.8 10.9 %collective-permute-start.45 = (f32[128,128]{1,0:T(8,128)S(1)}, f32[128,128]{1,0:T(8,128)S(1)}, u32[]{:S(2)}, u32[]{:S(2)}) collective-permute-start(f32[128,128]{1,0:T(8,128)S(1)} %get-tuple-element.16), channel_id=1, source_target_pairs={{1,0},{2,1},{3,2},{4,3},{5,4},{6,5},{7,6},{9,8},{10,9},{11,10},{12... | collective-permute-start | bytes 196616 | tf_op jit(solution)/shard_map/ppermute | solution.py:34
  532.1 13.8 %collective-permute-start.44 = (f32[128,128]{1,0:T(8,128)S(1)}, f32[128,128]{1,0:T(8,128)S(1)}, u32[]{:S(2)}, u32[]{:S(2)}) collective-permute-start(f32[128,128]{1,0:T(8,128)S(1)} %get-tuple-element.14), channel_id=1, source_target_pairs={{0,1},{1,2},{2,3},{3,4},{4,5},{5,6},{6,7},{8,9},{9,10},{10,11},{11... | collective-permute-start | bytes 196616 | tf_op jit(solution)/shard_map/ppermute | solution.py:34
  535.2 10.8 %collective-permute-start.43 = (f32[128,128]{1,0:T(8,128)S(1)}, f32[128,128]{1,0:T(8,128)S(1)}, u32[]{:S(2)}, u32[]{:S(2)}) collective-permute-start(f32[128,128]{1,0:T(8,128)S(1)} %get-tuple-element.15), channel_id=1, source_target_pairs={{8,0},{16,8},{24,16},{32,24},{40,32},{48,40},{56,48},{64,56},{72,6... | collective-permute-start | bytes 196616 | tf_op jit(solution)/shard_map/ppermute | solution.py:34
  539.8 8.9 %collective-permute-start.42 = (f32[128,128]{1,0:T(8,128)S(1)}, f32[128,128]{1,0:T(8,128)S(1)}, u32[]{:S(2)}, u32[]{:S(2)}) collective-permute-start(f32[128,128]{1,0:T(8,128)S(1)} %get-tuple-element.13), channel_id=1, source_target_pairs={{0,8},{8,16},{16,24},{24,32},{32,40},{40,48},{48,56},{56,64},{64,7... | collective-permute-start | bytes 196616 | tf_op jit(solution)/shard_map/ppermute | solution.py:34
  541.7 7.6 %collective-permute-start.47 = (bf16[2048,128]{1,0:T(8,128)(2,1)S(1)}, bf16[2048,128]{1,0:T(8,128)(2,1)S(1)}, u32[]{:S(2)}, u32[]{:S(2)}) collective-permute-start(bf16[2048,128]{1,0:T(8,128)(2,1)S(1)} %all_gather.7), channel_id=1, source_target_pairs={{0,7},{1,0},{2,1},{3,2},{4,3},{5,4},{6,5},{7,6},{8,15},{9,8},{10,9... | collective-permute-start | bytes 1572872 | tf_op jit(solution)/shard_map/ppermute | solution.py:23
  545.8 9.8 %collective-permute-start.48 = (bf16[2048,128]{1,0:T(8,128)(2,1)S(1)}, bf16[2048,128]{1,0:T(8,128)(2,1)S(1)}, u32[]{:S(2)}, u32[]{:S(2)}) collective-permute-start(bf16[2048,128]{1,0:T(8,128)(2,1)S(1)} %collective-permute-done.46), channel_id=1, source_target_pairs={{0,1},{1,2},{2,3},{3,4},{4,5},{5,6},{6,7},{7,0},{8,9},{9,10},{10,1... | collective-permute-start | bytes 1572872 | tf_op jit(solution)/shard_map/ppermute | solution.py:18
  549.4 9.8 %collective-permute-start.49 = (bf16[2048,128]{1,0:T(8,128)(2,1)S(1)}, bf16[2048,128]{1,0:T(8,128)(2,1)S(1)}, u32[]{:S(2)}, u32[]{:S(2)}) collective-permute-start(bf16[2048,128]{1,0:T(8,128)(2,1)S(1)} %collective-permute-done.47), channel_id=1, source_target_pairs={{0,7},{1,0},{2,1},{3,2},{4,3},{5,4},{6,5},{7,6},{8,15},{9,8},{10,9... | collective-permute-start | bytes 1572872 | tf_op jit(solution)/shard_map/ppermute | solution.py:23
  555.6 9.8 %collective-permute-start.50 = (bf16[2048,128]{1,0:T(8,128)(2,1)S(1)}, bf16[2048,128]{1,0:T(8,128)(2,1)S(1)}, u32[]{:S(2)}, u32[]{:S(2)}) collective-permute-start(bf16[2048,128]{1,0:T(8,128)(2,1)S(1)} %collective-permute-done.48), channel_id=1, source_target_pairs={{0,1},{1,2},{2,3},{3,4},{4,5},{5,6},{6,7},{7,0},{8,9},{9,10},{10,1... | collective-permute-start | bytes 1572872 | tf_op jit(solution)/shard_map/ppermute | solution.py:18
  559.2 9.8 %collective-permute-start.51 = (bf16[2048,128]{1,0:T(8,128)(2,1)S(1)}, bf16[2048,128]{1,0:T(8,128)(2,1)S(1)}, u32[]{:S(2)}, u32[]{:S(2)}) collective-permute-start(bf16[2048,128]{1,0:T(8,128)(2,1)S(1)} %collective-permute-done.49), channel_id=1, source_target_pairs={{0,7},{1,0},{2,1},{3,2},{4,3},{5,4},{6,5},{7,6},{8,15},{9,8},{10,9... | collective-permute-start | bytes 1572872 | tf_op jit(solution)/shard_map/ppermute | solution.py:23
  565.4 9.8 %collective-permute-start.52 = (bf16[2048,128]{1,0:T(8,128)(2,1)S(1)}, bf16[2048,128]{1,0:T(8,128)(2,1)S(1)}, u32[]{:S(2)}, u32[]{:S(2)}) collective-permute-start(bf16[2048,128]{1,0:T(8,128)(2,1)S(1)} %collective-permute-done.50), channel_id=1, source_target_pairs={{0,1},{1,2},{2,3},{3,4},{4,5},{5,6},{6,7},{7,0},{8,9},{9,10},{10,1... | collective-permute-start | bytes 1572872 | tf_op jit(solution)/shard_map/ppermute | solution.py:18
  584.6 12.0 %collective-permute-start.56 = (bf16[128,128]{1,0:T(8,128)(2,1)S(1)}, bf16[128,128]{1,0:T(8,128)(2,1)S(1)}, u32[]{:S(2)}, u32[]{:S(2)}) collective-permute-start(bf16[128,128]{1,0:T(8,128)(2,1)S(1)} %get-tuple-element.24), channel_id=1, source_target_pairs={{1,0},{2,1},{3,2},{4,3},{5,4},{6,5},{7,6},{9,8},{10,9},{11,10},{12... | collective-permute-start | bytes 98312 | tf_op jit(solution)/shard_map/ppermute | solution.py:34
  585.9 10.7 %collective-permute-start.55 = (bf16[128,128]{1,0:T(8,128)(2,1)S(1)}, bf16[128,128]{1,0:T(8,128)(2,1)S(1)}, u32[]{:S(2)}, u32[]{:S(2)}) collective-permute-start(bf16[128,128]{1,0:T(8,128)(2,1)S(1)} %get-tuple-element.22), channel_id=1, source_target_pairs={{0,1},{1,2},{2,3},{3,4},{4,5},{5,6},{6,7},{8,9},{9,10},{10,11},{11... | collective-permute-start | bytes 98312 | tf_op jit(solution)/shard_map/ppermute | solution.py:34
  589.0 7.7 %collective-permute-start.54 = (bf16[128,128]{1,0:T(8,128)(2,1)S(1)}, bf16[128,128]{1,0:T(8,128)(2,1)S(1)}, u32[]{:S(2)}, u32[]{:S(2)}) collective-permute-start(bf16[128,128]{1,0:T(8,128)(2,1)S(1)} %get-tuple-element.23), channel_id=1, source_target_pairs={{8,0},{16,8},{24,16},{32,24},{40,32},{48,40},{56,48},{64,56},{72,6... | collective-permute-start | bytes 98312 | tf_op jit(solution)/shard_map/ppermute | solution.py:34
  594.7 7.9 %collective-permute-start.53 = (bf16[128,128]{1,0:T(8,128)(2,1)S(1)}, bf16[128,128]{1,0:T(8,128)(2,1)S(1)}, u32[]{:S(2)}, u32[]{:S(2)}) collective-permute-start(bf16[128,128]{1,0:T(8,128)(2,1)S(1)} %get-tuple-element.21), channel_id=1, source_target_pairs={{0,8},{8,16},{16,24},{24,32},{32,40},{40,48},{48,56},{56,64},{64,7... | collective-permute-start | bytes 98312 | tf_op jit(solution)/shard_map/ppermute | solution.py:34
  613.8 7.0 collective-permute-start.59
  626.3 7.0 collective-permute-start.61
  645.0 9.4 %collective-permute-start.64 = (f32[2,128]{1,0:T(2,128)S(1)}, f32[2,128]{1,0:T(2,128)S(1)}, u32[]{:S(2)}, u32[]{:S(2)}) collective-permute-start(f32[2,128]{1,0:T(2,128)S(1)} %add.389), channel_id=1, source_target_pairs={{0,128},{8,136},{16,144},{24,152},{32,160},{40,168},{48,176},{56,1... | collective-permute-start | bytes 3080 | tf_op jit(solution)/shard_map/ppermute | solution.py:51
  654.4 14.2 %collective-permute-start.65 = (f32[2,128]{1,0:T(2,128)S(1)}, f32[2,128]{1,0:T(2,128)S(1)}, u32[]{:S(2)}, u32[]{:S(2)}) collective-permute-start(f32[2,128]{1,0:T(2,128)S(1)} %add.390), channel_id=1, source_target_pairs={{0,256},{8,264},{16,272},{24,280},{32,288},{40,296},{48,304},{56,3... | collective-permute-start | bytes 3080 | tf_op jit(solution)/shard_map/ppermute | solution.py:51
  677.1 7.0 collective-permute-start.68
  708.3 9.4 %collective-permute-start.73 = (f32[128]{0:T(128)S(1)}, f32[128]{0:T(128)S(1)}, u32[]{:S(2)}, u32[]{:S(2)}) collective-permute-start(f32[128]{0:T(128)S(1)} %add.399), channel_id=1, source_target_pairs={{0,128},{8,136},{16,144},{24,152},{32,160},{40,168},{48,176},{56,1... | collective-permute-start | bytes 1544 | tf_op jit(solution)/shard_map/ppermute | solution.py:51
  717.7 14.2 %collective-permute-start.74 = (f32[128]{0:T(128)S(1)}, f32[128]{0:T(128)S(1)}, u32[]{:S(2)}, u32[]{:S(2)}) collective-permute-start(f32[128]{0:T(128)S(1)} %add.400), channel_id=1, source_target_pairs={{0,256},{8,264},{16,272},{24,280},{32,288},{40,296},{48,304},{56,3... | collective-permute-start | bytes 1544 | tf_op jit(solution)/shard_map/ppermute | solution.py:51
  (34 other events, 801.1 us)
